TPU v7x, 256 devices: a whole 4x4x8 slice. The times are simulated.
256 devices in a mesh: ctx: 64 (over z, x, core), head: 4 (over y).
Axes of the slice: x: 4, y: 4, z: 8, core: 2. Of those that a mesh axis runs over, the one named last changes fastest.
Arguments:
- queries: bfloat16 [8192, 32, 128], P('ctx', 'head'), may hold values from -14 to 14
- keys: bfloat16 [8192, 32, 128], P('ctx', 'head'), may hold values from -14 to 14
- values: bfloat16 [8192, 32, 128], P('ctx', 'head'), may hold values from -6 to 6
- gain: float32 [32, 128], P('head'), may hold values from 0.1 to 1.9
- doc_lengths: int32 [64], replicated, may hold values from 1 to 2048, 8192 in all
- cotangent: bfloat16 [8192, 32, 128], P('ctx', 'head'), may hold values from -6 to 6
Outputs:
- mixed: bfloat16 [8192, 32, 128], P('ctx', 'head')
- query_grad: bfloat16 [8192, 32, 128], P('ctx', 'head')
- key_grad: bfloat16 [8192, 32, 128], P('ctx', 'head')
- value_grad: bfloat16 [8192, 32, 128], P('ctx', 'head')
All inputs are finite; a program needn't handle non-finite values.
Results may differ from a plain program's by a relative error of at most 0.0054.
Values may be sent and summed in bfloat16 or wider, within the bound.
No kernel may reach another device: no remote copies, remote signals or barrier semaphores. Data moves between devices by JAX's collectives and lax.ppermute only.
A program may use at most 128 MiB of HBM per device.

v0:
```python
import jax
import jax.numpy as jnp
from jax import lax
from jax.sharding import PartitionSpec as P

SPAN = 2
MAXDOC = 2048
neg_large = -1e30
norm_eps = 1e-06


def from_behind(x, axis, by):
    devices = lax.axis_size(axis)
    pairs = [(i, i + by) for i in range(devices) if 0 <= i + by < devices]
    return lax.ppermute(x, axis, pairs)


def tile_state(keys_t, values_t, doc_lengths, start):
    tile = keys_t.shape[0]
    docs = doc_index(doc_lengths, start + jnp.arange(tile, dtype=jnp.int32))
    keep = (docs == docs[tile - 1])[:, None, None]
    return narrow("uhd,uhe->hde", jnp.where(keep, keys_t, jnp.zeros_like(keys_t)), values_t)


def fold_states(pieces, flags):
    total = pieces[0]
    for piece, flag in zip(pieces[1:], flags[1:]):
        total = piece + (1.0 - flag) * total
    return total


def front_flags(doc_lengths, spans, tile):
    low = jnp.stack([lo * tile - 1 for lo, hi in spans])
    high = jnp.stack([hi * tile + tile - 1 for lo, hi in spans])
    docs = doc_index(doc_lengths, jnp.concatenate([low, high]).astype(jnp.int32))
    count = len(spans)
    return (docs[:count] != docs[count:]).astype(jnp.float32)


def back_flags(doc_lengths, spans, tile):
    low = jnp.stack([lo * tile for lo, hi in spans])
    high = jnp.stack([hi * tile + tile for lo, hi in spans])
    docs = doc_index(doc_lengths, jnp.concatenate([low, high]).astype(jnp.int32))
    count = len(spans)
    return (docs[:count] != docs[count:]).astype(jnp.float32)


def wide(form, left, right):
    return jnp.einsum(form, left, right, precision=lax.Precision.HIGHEST)


def narrow(form, left, right):
    return jnp.einsum(form, left, right, preferred_element_type=jnp.float32)


def doc_index(doc_lengths, positions):
    starts = jnp.cumsum(doc_lengths) - doc_lengths
    return jnp.sum((starts[None, :] <= positions[:, None]).astype(jnp.int32), axis=1) - 1


def one_doc(doc_lengths, position):
    return doc_index(doc_lengths, jnp.reshape(position, (1,)))[0]


def masked_scores(query_block, key_block, mask, scale):
    raw = narrow("thd,uhd->htu", query_block, key_block) * scale
    return jnp.where(mask[None], raw, neg_large)


def key_terms(dscores, weights, query_block, grad_block, scale):
    key_part = narrow("htu,thd->uhd", dscores, query_block) * scale
    value_part = narrow("htu,thd->uhd", weights, grad_block)
    return (key_part, value_part)


def per_device(queries, keys, values, gain, doc_lengths, cotangent):
    tile, heads, width = queries.shape
    features = heads * lax.axis_size("head") * width
    scale = width ** (-0.5)
    base = lax.axis_index("ctx") * tile
    offsets = jnp.arange(tile, dtype=jnp.int32)
    own_pos = base + offsets
    own_doc = doc_index(doc_lengths, own_pos)
    prev_doc = one_doc(doc_lengths, base - 1)
    next_doc = one_doc(doc_lengths, base + tile)
    pair = jnp.stack([keys, values])
    arrived = [from_behind(pair, "ctx", shift) for shift in range(SPAN, 0, -1)]
    key_tiles = [piece[0] for piece in arrived] + [keys]
    value_tiles = [piece[1] for piece in arrived] + [values]
    masks = []
    for position in range(SPAN + 1):
        key_pos = base - (SPAN - position) * tile + offsets
        key_doc = doc_index(doc_lengths, key_pos)
        masks.append(
            (own_doc[:, None] == key_doc[None, :]) & (key_pos[None, :] <= own_pos[:, None])
        )
    score_list = [
        masked_scores(queries, key_tiles[position], masks[position], scale)
        for position in range(SPAN + 1)
    ]
    top = score_list[0].max(axis=-1)
    for position in range(1, SPAN + 1):
        top = jnp.maximum(top, score_list[position].max(axis=-1))
    total = jnp.zeros((heads, tile), jnp.float32)
    for position in range(SPAN + 1):
        total = total + jnp.sum(jnp.exp(score_list[position] - top[..., None]), axis=-1)
    log_total = top + jnp.log(total)
    prob_list = []
    weight_list = []
    soft_out = jnp.zeros((tile, heads, width), jnp.float32)
    for position in range(SPAN + 1):
        probs = jnp.exp(score_list[position] - log_total[..., None])
        weights = probs.astype(jnp.bfloat16)
        prob_list.append(probs)
        weight_list.append(weights)
        soft_out = soft_out + narrow("htu,uhd->thd", weights, value_tiles[position])
    same_tile = masks[SPAN].astype(jnp.float32)
    carried_prev = (own_doc == prev_doc).astype(jnp.float32)
    carried_next = (own_doc == next_doc).astype(jnp.float32)
    keep_first = (own_doc == own_doc[0])[:, None, None]
    query_wide = queries.astype(jnp.float32)
    attend = (narrow("thd,uhd->htu", queries, keys) * same_tile).astype(jnp.bfloat16)
    place = lax.axis_index("ctx")
    need = min(-(-MAXDOC // tile), lax.axis_size("ctx"))
    group = SPAN + 2
    rounds = -(-need // group)
    own_state = tile_state(keys, values, doc_lengths, base)
    far_states = [from_behind(own_state, "ctx", shift) for shift in range(group - 1, SPAN, -1)]
    near_states = [
        tile_state(
            key_tiles[position], value_tiles[position], doc_lengths, base - (SPAN - position) * tile
        )
        for position in range(SPAN)
    ]
    group_spans = [(place - shift, place - shift) for shift in range(group - 1, -1, -1)]
    group_state = fold_states(
        far_states + near_states + [own_state], front_flags(doc_lengths, group_spans, tile)
    )
    shifts = [1 + group * k for k in range(rounds - 1, -1, -1)]
    window_spans = [(place - shift - group + 1, place - shift) for shift in shifts]
    incoming = fold_states(
        [from_behind(group_state, "ctx", shift) for shift in shifts],
        front_flags(doc_lengths, window_spans, tile),
    )
    linear_out = (
        narrow("htu,uhd->thd", attend, values)
        + wide("thd,hde->the", query_wide, incoming) * carried_prev[:, None, None]
    )
    squares = lax.psum(jnp.sum(linear_out * linear_out, axis=(1, 2)), "head")
    inverse = lax.rsqrt(squares / features + norm_eps)
    mixed = (linear_out * inverse[:, None, None] * gain[None] + soft_out).astype(jnp.bfloat16)
    grad_wide = cotangent.astype(jnp.float32)
    weighted = grad_wide * gain[None]
    projection = lax.psum(jnp.sum(weighted * linear_out, axis=(1, 2)), "head")
    inner = (
        inverse[:, None, None] * weighted
        - linear_out * (inverse**3 * projection / features)[:, None, None]
    ).astype(jnp.bfloat16)
    row_dot = jnp.sum(grad_wide * soft_out, axis=-1).T
    query_soft = jnp.zeros((tile, heads, width), jnp.float32)
    dscore_list = []
    for position in range(SPAN + 1):
        dprobs = narrow("thd,uhd->htu", cotangent, value_tiles[position])
        dscores = (prob_list[position] * (dprobs - row_dot[..., None])).astype(jnp.bfloat16)
        query_soft = query_soft + narrow("htu,uhd->thd", dscores, key_tiles[position]) * scale
        dscore_list.append(dscores)
    inner_wide = inner.astype(jnp.float32)
    back = (narrow("thd,uhd->htu", inner, values) * same_tile).astype(jnp.bfloat16)
    query_linear = (
        narrow("htu,uhd->thd", back, keys)
        + wide("the,hde->thd", inner_wide, incoming) * carried_prev[:, None, None]
    )
    tile_sum = narrow(
        "thd,the->hde", jnp.where(keep_first, queries, jnp.zeros_like(queries)), inner
    )
    back_states = [from_behind(tile_sum, "ctx", -shift) for shift in range(group - 1, 0, -1)] + [
        tile_sum
    ]
    back_spans = [(place + shift, place + shift) for shift in range(group - 1, -1, -1)]
    back_group = fold_states(back_states, back_flags(doc_lengths, back_spans, tile))
    back_window = [(place + shift, place + shift + group - 1) for shift in shifts]
    later = fold_states(
        [from_behind(back_group, "ctx", -shift) for shift in shifts],
        back_flags(doc_lengths, back_window, tile),
    )
    key_linear = (
        narrow("htu,thd->uhd", back, queries)
        + wide("uhe,hde->uhd", values.astype(jnp.float32), later) * carried_next[:, None, None]
    )
    value_linear = (
        narrow("htu,the->uhe", attend, inner)
        + wide("uhd,hde->uhe", keys.astype(jnp.float32), later) * carried_next[:, None, None]
    )
    parts = [
        key_terms(dscore_list[position], weight_list[position], queries, cotangent, scale)
        for position in range(SPAN + 1)
    ]
    key_soft, value_soft = parts[SPAN]
    for shift in range(1, SPAN + 1):
        sent = jnp.stack([parts[SPAN - shift][0], parts[SPAN - shift][1]])
        returned = from_behind(sent.astype(jnp.bfloat16), "ctx", -shift).astype(sent.dtype)
        key_soft = key_soft + returned[0]
        value_soft = value_soft + returned[1]
    query_grad = (query_linear + query_soft).astype(jnp.bfloat16)
    key_grad = (key_linear + key_soft).astype(jnp.bfloat16)
    value_grad = (value_linear + value_soft).astype(jnp.bfloat16)
    return (mixed, query_grad, key_grad, value_grad)


def solution(mesh):
    placed = (
        P("ctx", "head", None),
        P("ctx", "head", None),
        P("ctx", "head", None),
        P("head", None),
        P(),
        P("ctx", "head", None),
    )
    return jax.shard_map(
        per_device,
        mesh=mesh,
        in_specs=placed,
        out_specs=(
            P("ctx", "head", None),
            P("ctx", "head", None),
            P("ctx", "head", None),
            P("ctx", "head", None),
        ),
        check_vma=False,
    )
```

profile of v0, /device:TPU:67, one launch (start us, length us, event | category | flops | bytes accessed | tf_op | source)
XLA Modules:
  0.0 234.4 jit_solution(17210112491992321629)
XLA Ops:
  0.6 1.1 copy_bitcast_fusion
  1.8 0.8 pad_maximum_fusion
  2.6 3.1 %collective-permute-start.1 = (bf16[2,128,8,128]{3,1,2,0:T(8,128)(2,1)}, bf16[2,128,8,128]{3,1,2,0:T(8,128)(2,1)S(1)}, u32[]{:S(2)}, u32[]{:S(2)}) collective-permute-start(bf16[2,128,8,128]{3,1,2,0:T(8,128)(2,1)} %pad_maximum_fusion), channel_id=1, source_target_pairs={{0,8},{4,12},{8,16},{12,20},{16,24},{20,28},{24,32},{28,36},{32,40... | collective-permute-start | bytes 1572872 | tf_op jit(solution)/shard_map/ppermute | solution.py:15
  5.7 3.7 %collective-permute-start = (bf16[2,128,8,128]{3,1,2,0:T(8,128)(2,1)}, bf16[2,128,8,128]{3,1,2,0:T(8,128)(2,1)S(1)}, u32[]{:S(2)}, u32[]{:S(2)}) collective-permute-start(bf16[2,128,8,128]{3,1,2,0:T(8,128)(2,1)} %pad_maximum_fusion), channel_id=1, source_target_pairs={{0,4},{4,8},{8,12},{12,16},{16,20},{20,24},{24,28},{28,32},{32,36}... | collective-permute-start | bytes 1572872 | tf_op jit(solution)/shard_map/ppermute | solution.py:15
  9.5 0.6 copy-done.15
  10.4 0.7 fusion.105
  11.9 0.6 fusion.116
  13.2 1.2 compare_convert_fusion
  14.4 0.3 fusion.61
  14.8 3.2 %collective-permute-start.2 = (f32[8,128,128]{2,1,0:T(8,128)S(1)}, f32[8,128,128]{2,1,0:T(8,128)}, u32[]{:S(2)}, u32[]{:S(2)}) collective-permute-start(f32[8,128,128]{2,1,0:T(8,128)S(1)} %fusion.61), channel_id=1, source_target_pairs={{0,12},{4,16},{8,20},{12,24},{16,28},{20,32},{24,36},{28,40},{32,4... | collective-permute-start | bytes 1572872 | tf_op jit(solution)/shard_map/ppermute | solution.py:15
  18.0 0.7 slice.82
  18.8 0.6 slice.79
  20.1 0.6 fusion.118
  20.7 0.7 fusion.117
  21.5 0.7 fusion.115
  22.2 1.3 broadcast_compare_fusion.1
  23.5 0.7 fusion.114
  24.4 0.7 copy-done.1
  25.1 0.3 fusion.56
  33.0 0.3 convolution_bitcast_fusion.4
  33.3 1.6 fusion.17
  35.0 0.4 fusion.19
  35.3 5.5 %collective-permute-start.3 = (f32[8,128,128]{2,1,0:T(8,128)S(1)}, f32[8,128,128]{2,1,0:T(8,128)S(1)}, u32[]{:S(2)}, u32[]{:S(2)}) collective-permute-start(f32[8,128,128]{2,1,0:T(8,128)S(1)} %fusion.19), channel_id=1, source_target_pairs={{0,4},{4,8},{8,12},{12,16},{16,20},{20,24},{24,28},{28,32},{32,36}... | collective-permute-start | bytes 1572872 | tf_op jit(solution)/shard_map/ppermute | solution.py:15
  40.8 5.5 %collective-permute-start.4 = (f32[8,128,128]{2,1,0:T(8,128)S(1)}, f32[8,128,128]{2,1,0:T(8,128)S(1)}, u32[]{:S(2)}, u32[]{:S(2)}) collective-permute-start(f32[8,128,128]{2,1,0:T(8,128)S(1)} %fusion.19), channel_id=1, source_target_pairs={{0,20},{4,24},{8,28},{12,32},{16,36},{20,40},{24,44},{28,48},{32,5... | collective-permute-start | bytes 1572872 | tf_op jit(solution)/shard_map/ppermute | solution.py:15
  46.4 12.2 %collective-permute-start.5 = (f32[8,128,128]{2,1,0:T(8,128)S(1)}, f32[8,128,128]{2,1,0:T(8,128)S(1)}, u32[]{:S(2)}, u32[]{:S(2)}) collective-permute-start(f32[8,128,128]{2,1,0:T(8,128)S(1)} %fusion.19), channel_id=1, source_target_pairs={{0,36},{4,40},{8,44},{12,48},{16,52},{20,56},{24,60},{28,64},{32,6... | collective-permute-start | bytes 1572872 | tf_op jit(solution)/shard_map/ppermute | solution.py:15
  58.5 1.9 collective-permute-start.6
  61.4 0.3 convolution_bitcast_fusion.3
  61.7 0.6 copy-done
  62.3 0.9 fusion.42
  63.3 0.9 fusion.41
  64.2 1.0 convolution_bitcast_fusion
  65.6 0.8 copy-done.7
  66.6 4.2 %collective-permute-done.5 = f32[8,128,128]{2,1,0:T(8,128)S(1)} collective-permute-done((f32[8,128,128]{2,1,0:T(8,128)S(1)}, f32[8,128,128]{2,1,0:T(8,128)S(1)}, u32[]{:S(2)}, u32[]{:S(2)}) %collective-permute-start.5) | collective-permute-done | bytes 524320 | tf_op jit(solution)/shard_map/ppermute | solution.py:15
  70.8 11.6 %collective-permute-done.6 = f32[8,128,128]{2,1,0:T(8,128)S(1)} collective-permute-done((f32[8,128,128]{2,1,0:T(8,128)S(1)}, f32[8,128,128]{2,1,0:T(8,128)S(1)}, u32[]{:S(2)}, u32[]{:S(2)}) %collective-permute-start.6) | collective-permute-done | bytes 524320 | tf_op jit(solution)/shard_map/ppermute | solution.py:15
  82.5 0.6 copy-done.14
  83.1 1.4 fusion.47
  84.5 8.7 %all-reduce = (f32[128]{0:T(128)S(1)}, f32[128]{0:T(128)S(1)}) all-reduce(f32[128]{0:T(128)S(1)} %get-tuple-element.17, f32[128]{0:T(128)S(1)} %get-tuple-element.16), channel_id=1, replica_groups=mesh['ctx'=64,'head'=4] {'head'}, use_global_device_ids=true, to_apply=%region_8.9 | all-reduce | flops 256 | bytes 2048 | tf_op jit(solution)/shard_map/psum | solution.py:149
  93.2 1.3 fusion.46
  94.8 0.4 fusion.57
  95.1 6.3 %collective-permute-start.7 = (f32[8,128,128]{2,1,0:T(8,128)S(1)}, f32[8,128,128]{2,1,0:T(8,128)S(1)}, u32[]{:S(2)}, u32[]{:S(2)}) collective-permute-start(f32[8,128,128]{2,1,0:T(8,128)S(1)} %fusion.57), channel_id=1, source_target_pairs={{4,0},{8,4},{12,8},{16,12},{20,16},{24,20},{28,24},{32,28},{36,32}... | collective-permute-start | bytes 1572872 | tf_op jit(solution)/shard_map/ppermute | solution.py:15
  101.4 2.5 %collective-permute-start.8 = (f32[8,128,128]{2,1,0:T(8,128)S(1)}, f32[8,128,128]{2,1,0:T(8,128)S(1)}, u32[]{:S(2)}, u32[]{:S(2)}) collective-permute-start(f32[8,128,128]{2,1,0:T(8,128)S(1)} %fusion.57), channel_id=1, source_target_pairs={{8,0},{12,4},{16,8},{20,12},{24,16},{28,20},{32,24},{36,28},{40,32... | collective-permute-start | bytes 1572872 | tf_op jit(solution)/shard_map/ppermute | solution.py:15
  103.9 18.1 %collective-permute-start.9 = (f32[8,128,128]{2,1,0:T(8,128)S(1)}, f32[8,128,128]{2,1,0:T(8,128)S(1)}, u32[]{:S(2)}, u32[]{:S(2)}) collective-permute-start(f32[8,128,128]{2,1,0:T(8,128)S(1)} %fusion.57), channel_id=1, source_target_pairs={{12,0},{16,4},{20,8},{24,12},{28,16},{32,20},{36,24},{40,28},{44,3... | collective-permute-start | bytes 1572872 | tf_op jit(solution)/shard_map/ppermute | solution.py:15
  122.3 0.7 fusion.27
  123.0 0.4 copy-done.8
  123.9 0.7 copy-done.13
  124.7 2.1 collective-permute-start.15
  126.8 0.3 fusion.34
  127.3 0.7 copy-done.12
  128.1 2.3 collective-permute-start.14
  131.0 0.3 fusion.35
  131.6 8.1 %collective-permute-done.9 = f32[8,128,128]{2,1,0:T(8,128)S(1)} collective-permute-done((f32[8,128,128]{2,1,0:T(8,128)S(1)}, f32[8,128,128]{2,1,0:T(8,128)S(1)}, u32[]{:S(2)}, u32[]{:S(2)}) %collective-permute-start.9) | collective-permute-done | bytes 524320 | tf_op jit(solution)/shard_map/ppermute | solution.py:15
  139.9 8.1 %collective-permute-start.10 = (f32[8,128,128]{2,1,0:T(8,128)S(1)}, f32[8,128,128]{2,1,0:T(8,128)S(1)}, u32[]{:S(2)}, u32[]{:S(2)}) collective-permute-start(f32[8,128,128]{2,1,0:T(8,128)S(1)} %multiply_add_fusion.1), channel_id=1, source_target_pairs={{4,0},{8,4},{12,8},{16,12},{20,16},{24,20},{28,24},{32,28},{36,32}... | collective-permute-start | bytes 1572872 | tf_op jit(solution)/shard_map/ppermute | solution.py:15
  148.0 16.8 %collective-permute-start.11 = (f32[8,128,128]{2,1,0:T(8,128)S(1)}, f32[8,128,128]{2,1,0:T(8,128)S(1)}, u32[]{:S(2)}, u32[]{:S(2)}) collective-permute-start(f32[8,128,128]{2,1,0:T(8,128)S(1)} %multiply_add_fusion.1), channel_id=1, source_target_pairs={{20,0},{24,4},{28,8},{32,12},{36,16},{40,20},{44,24},{48,28},{52,3... | collective-permute-start | bytes 1572872 | tf_op jit(solution)/shard_map/ppermute | solution.py:15
  164.8 1.9 collective-permute-start.12
  166.7 2.1 collective-permute-start.13
  169.1 0.9 copy.213
  170.0 0.9 copy.214
  171.5 1.1 collective-permute-done.10
  172.6 28.9 %collective-permute-done.11 = f32[8,128,128]{2,1,0:T(8,128)S(1)} collective-permute-done((f32[8,128,128]{2,1,0:T(8,128)S(1)}, f32[8,128,128]{2,1,0:T(8,128)S(1)}, u32[]{:S(2)}, u32[]{:S(2)}) %collective-permute-start.11) | collective-permute-done | bytes 524320 | tf_op jit(solution)/shard_map/ppermute | solution.py:15
  201.5 29.7 %collective-permute-done.13 = f32[8,128,128]{2,1,0:T(8,128)S(1)} collective-permute-done((f32[8,128,128]{2,1,0:T(8,128)S(1)}, f32[8,128,128]{2,1,0:T(8,128)S(1)}, u32[]{:S(2)}, u32[]{:S(2)}) %collective-permute-start.13) | collective-permute-done | bytes 524320 | tf_op jit(solution)/shard_map/ppermute | solution.py:15
  231.3 0.7 fusion.31
  232.0 0.9 copy.215
  233.0 0.4 fusion.32
  233.5 0.9 copy.216
  (83 shorter events, 6.8 us)
Async XLA Ops:
  1.8 12.6 %copy-start.2 = (bf16[128,8,128]{2,1,0:T(8,128)(2,1)S(1)}, bf16[128,8,128]{2,1,0:T(8,128)(2,1)}, u32[]{:S(2)}) copy-start(bf16[128,8,128]{2,1,0:T(8,128)(2,1)} %param.8) | copy-start | bytes 786436
  1.8 12.6 %copy-start.3 = (bf16[128,8,128]{2,1,0:T(8,128)(2,1)S(1)}, bf16[128,8,128]{2,1,0:T(8,128)(2,1)}, u32[]{:S(2)}) copy-start(bf16[128,8,128]{2,1,0:T(8,128)(2,1)} %param.7) | copy-start | bytes 786436
  2.6 30.7 %collective-permute-start.1 = (bf16[2,128,8,128]{3,1,2,0:T(8,128)(2,1)}, bf16[2,128,8,128]{3,1,2,0:T(8,128)(2,1)S(1)}, u32[]{:S(2)}, u32[]{:S(2)}) collective-permute-start(bf16[2,128,8,128]{3,1,2,0:T(8,128)(2,1)} %pad_maximum_fusion), channel_id=1, source_target_pairs={{0,8},{4,12},{8,16},{12,20},{16,24},{20,28},{24,32},{28,36},{32,40... | collective-permute-start | bytes 1572872 | tf_op jit(solution)/shard_map/ppermute | solution.py:15
  5.7 29.2 %collective-permute-start = (bf16[2,128,8,128]{3,1,2,0:T(8,128)(2,1)}, bf16[2,128,8,128]{3,1,2,0:T(8,128)(2,1)S(1)}, u32[]{:S(2)}, u32[]{:S(2)}) collective-permute-start(bf16[2,128,8,128]{3,1,2,0:T(8,128)(2,1)} %pad_maximum_fusion), channel_id=1, source_target_pairs={{0,4},{4,8},{8,12},{12,16},{16,20},{20,24},{24,28},{28,32},{32,36}... | collective-permute-start | bytes 1572872 | tf_op jit(solution)/shard_map/ppermute | solution.py:15
  9.4 0.7 copy-start.15
  14.8 18.6 %collective-permute-start.2 = (f32[8,128,128]{2,1,0:T(8,128)S(1)}, f32[8,128,128]{2,1,0:T(8,128)}, u32[]{:S(2)}, u32[]{:S(2)}) collective-permute-start(f32[8,128,128]{2,1,0:T(8,128)S(1)} %fusion.61), channel_id=1, source_target_pairs={{0,12},{4,16},{8,20},{12,24},{16,28},{20,32},{24,36},{28,40},{32,4... | collective-permute-start | bytes 1572872 | tf_op jit(solution)/shard_map/ppermute | solution.py:15
  24.1 1.0 copy-start.1
  33.3 27.1 %copy-start.6 = (bf16[2,128,8,128]{3,1,2,0:T(8,128)(2,1)}, bf16[2,128,8,128]{3,1,2,0:T(8,128)(2,1)S(1)}, u32[]{:S(2)}) copy-start(bf16[2,128,8,128]{3,1,2,0:T(8,128)(2,1)S(1)} %collective-permute-done.1) | copy-start | bytes 1572868
  34.9 30.3 %copy-start.9 = (bf16[2,128,8,128]{3,1,2,0:T(8,128)(2,1)}, bf16[2,128,8,128]{3,1,2,0:T(8,128)(2,1)S(1)}, u32[]{:S(2)}) copy-start(bf16[2,128,8,128]{3,1,2,0:T(8,128)(2,1)S(1)} %collective-permute-done) | copy-start | bytes 1572868
  35.3 31.3 %collective-permute-start.3 = (f32[8,128,128]{2,1,0:T(8,128)S(1)}, f32[8,128,128]{2,1,0:T(8,128)S(1)}, u32[]{:S(2)}, u32[]{:S(2)}) collective-permute-start(f32[8,128,128]{2,1,0:T(8,128)S(1)} %fusion.19), channel_id=1, source_target_pairs={{0,4},{4,8},{8,12},{12,16},{16,20},{20,24},{24,28},{28,32},{32,36}... | collective-permute-start | bytes 1572872 | tf_op jit(solution)/shard_map/ppermute | solution.py:15
  40.8 25.8 %collective-permute-start.4 = (f32[8,128,128]{2,1,0:T(8,128)S(1)}, f32[8,128,128]{2,1,0:T(8,128)S(1)}, u32[]{:S(2)}, u32[]{:S(2)}) collective-permute-start(f32[8,128,128]{2,1,0:T(8,128)S(1)} %fusion.19), channel_id=1, source_target_pairs={{0,20},{4,24},{8,28},{12,32},{16,36},{20,40},{24,44},{28,48},{32,5... | collective-permute-start | bytes 1572872 | tf_op jit(solution)/shard_map/ppermute | solution.py:15
  46.4 24.5 %collective-permute-start.5 = (f32[8,128,128]{2,1,0:T(8,128)S(1)}, f32[8,128,128]{2,1,0:T(8,128)S(1)}, u32[]{:S(2)}, u32[]{:S(2)}) collective-permute-start(f32[8,128,128]{2,1,0:T(8,128)S(1)} %fusion.19), channel_id=1, source_target_pairs={{0,36},{4,40},{8,44},{12,48},{16,52},{20,56},{24,60},{28,64},{32,6... | collective-permute-start | bytes 1572872 | tf_op jit(solution)/shard_map/ppermute | solution.py:15
  58.5 23.9 %collective-permute-start.6 = (f32[8,128,128]{2,1,0:T(8,128)S(1)}, f32[8,128,128]{2,1,0:T(8,128)S(1)}, u32[]{:S(2)}, u32[]{:S(2)}) collective-permute-start(f32[8,128,128]{2,1,0:T(8,128)S(1)} %fusion.19), channel_id=1, source_target_pairs={{0,52},{4,56},{8,60},{12,64},{16,68},{20,72},{24,76},{28,80},{32,8... | collective-permute-start | bytes 1572872 | tf_op jit(solution)/shard_map/ppermute | solution.py:15
  61.4 1.0 copy-start
  65.3 1.0 copy-start.7
  82.4 0.7 copy-start.14
  82.5 1.9 copy-start.4
  95.1 27.2 %copy-start.5 = (f32[8,128,128]{2,1,0:T(8,128)S(1)}, f32[8,128,128]{2,1,0:T(8,128)}, u32[]{:S(2)}) copy-start(f32[8,128,128]{2,1,0:T(8,128)} %copy-done.4) | copy-start | bytes 1572868
  95.1 36.4 %collective-permute-start.7 = (f32[8,128,128]{2,1,0:T(8,128)S(1)}, f32[8,128,128]{2,1,0:T(8,128)S(1)}, u32[]{:S(2)}, u32[]{:S(2)}) collective-permute-start(f32[8,128,128]{2,1,0:T(8,128)S(1)} %fusion.57), channel_id=1, source_target_pairs={{4,0},{8,4},{12,8},{16,12},{20,16},{24,20},{28,24},{32,28},{36,32}... | collective-permute-start | bytes 1572872 | tf_op jit(solution)/shard_map/ppermute | solution.py:15
  101.4 30.2 %collective-permute-start.8 = (f32[8,128,128]{2,1,0:T(8,128)S(1)}, f32[8,128,128]{2,1,0:T(8,128)S(1)}, u32[]{:S(2)}, u32[]{:S(2)}) collective-permute-start(f32[8,128,128]{2,1,0:T(8,128)S(1)} %fusion.57), channel_id=1, source_target_pairs={{8,0},{12,4},{16,8},{20,12},{24,16},{28,20},{32,24},{36,28},{40,32... | collective-permute-start | bytes 1572872 | tf_op jit(solution)/shard_map/ppermute | solution.py:15
  103.9 35.8 %collective-permute-start.9 = (f32[8,128,128]{2,1,0:T(8,128)S(1)}, f32[8,128,128]{2,1,0:T(8,128)S(1)}, u32[]{:S(2)}, u32[]{:S(2)}) collective-permute-start(f32[8,128,128]{2,1,0:T(8,128)S(1)} %fusion.57), channel_id=1, source_target_pairs={{12,0},{16,4},{20,8},{24,12},{28,16},{32,20},{36,24},{40,28},{44,3... | collective-permute-start | bytes 1572872 | tf_op jit(solution)/shard_map/ppermute | solution.py:15
  122.3 1.0 copy-start.8
  123.7 1.0 copy-start.13
  124.6 2.1 copy-start.10
  124.7 42.1 %collective-permute-start.15 = (bf16[2,128,8,128]{3,1,2,0:T(8,128)(2,1)S(1)}, bf16[2,128,8,128]{3,1,2,0:T(8,128)(2,1)S(1)}, u32[]{:S(2)}, u32[]{:S(2)}) collective-permute-start(bf16[2,128,8,128]{3,1,2,0:T(8,128)(2,1)S(1)} %pad_maximum_fusion.2), channel_id=1, source_target_pairs={{8,0},{12,4},{16,8},{20,12},{24,16},{28,20},{32,24},{36,28},{40,32... | collective-permute-start | bytes 1572872 | tf_op jit(solution)/shard_map/ppermute | solution.py:15
  127.1 1.0 copy-start.12
  128.1 43.3 %collective-permute-start.14 = (bf16[2,128,8,128]{3,1,2,0:T(8,128)(2,1)S(1)}, bf16[2,128,8,128]{3,1,2,0:T(8,128)(2,1)S(1)}, u32[]{:S(2)}, u32[]{:S(2)}) collective-permute-start(bf16[2,128,8,128]{3,1,2,0:T(8,128)(2,1)S(1)} %pad_maximum_fusion.1), channel_id=1, source_target_pairs={{4,0},{8,4},{12,8},{16,12},{20,16},{24,20},{28,24},{32,28},{36,32}... | collective-permute-start | bytes 1572872 | tf_op jit(solution)/shard_map/ppermute | solution.py:15
  139.9 32.7 %collective-permute-start.10 = (f32[8,128,128]{2,1,0:T(8,128)S(1)}, f32[8,128,128]{2,1,0:T(8,128)S(1)}, u32[]{:S(2)}, u32[]{:S(2)}) collective-permute-start(f32[8,128,128]{2,1,0:T(8,128)S(1)} %multiply_add_fusion.1), channel_id=1, source_target_pairs={{4,0},{8,4},{12,8},{16,12},{20,16},{24,20},{28,24},{32,28},{36,32}... | collective-permute-start | bytes 1572872 | tf_op jit(solution)/shard_map/ppermute | solution.py:15
  148.0 53.5 %collective-permute-start.11 = (f32[8,128,128]{2,1,0:T(8,128)S(1)}, f32[8,128,128]{2,1,0:T(8,128)S(1)}, u32[]{:S(2)}, u32[]{:S(2)}) collective-permute-start(f32[8,128,128]{2,1,0:T(8,128)S(1)} %multiply_add_fusion.1), channel_id=1, source_target_pairs={{20,0},{24,4},{28,8},{32,12},{36,16},{40,20},{44,24},{48,28},{52,3... | collective-permute-start | bytes 1572872 | tf_op jit(solution)/shard_map/ppermute | solution.py:15
  164.8 36.7 %collective-permute-start.12 = (f32[8,128,128]{2,1,0:T(8,128)S(1)}, f32[8,128,128]{2,1,0:T(8,128)S(1)}, u32[]{:S(2)}, u32[]{:S(2)}) collective-permute-start(f32[8,128,128]{2,1,0:T(8,128)S(1)} %multiply_add_fusion.1), channel_id=1, source_target_pairs={{36,0},{40,4},{44,8},{48,12},{52,16},{56,20},{60,24},{64,28},{68,3... | collective-permute-start | bytes 1572872 | tf_op jit(solution)/shard_map/ppermute | solution.py:15
  166.7 64.4 %collective-permute-start.13 = (f32[8,128,128]{2,1,0:T(8,128)S(1)}, f32[8,128,128]{2,1,0:T(8,128)S(1)}, u32[]{:S(2)}, u32[]{:S(2)}) collective-permute-start(f32[8,128,128]{2,1,0:T(8,128)S(1)} %multiply_add_fusion.1), channel_id=1, source_target_pairs={{52,0},{56,4},{60,8},{64,12},{68,16},{72,20},{76,24},{80,28},{84,3... | collective-permute-start | bytes 1572872 | tf_op jit(solution)/shard_map/ppermute | solution.py:15
  232.0 1.0 copy-start.11
where the time goes:
time: 235 us; the launch traced here: 234 us
  starting transfers between devices  95.2 us (41%)
  waiting for transfers between devices  83.6 us (36%)
  local copies, waits for them, and re-layouts  14.9 us (6%)
  matrix products  14.3 us (6%)
  between operations  10.3 us (4%)
  blocking collectives  8.7 us (4%)
  other arithmetic  7.28 us (3%)
    ppermute x16, starting transfers between devices, from_behind(): return lax.ppermute(x, axis, pairs)  95.2 us
    ppermute x16, waiting for transfers between devices, from_behind(): return lax.ppermute(x, axis, pairs)  83.6 us
    dot_general x27, matrix products, narrow(): return jnp.einsum(form, left, right, preferred_element_type=jnp.float32)  11.1 us
    unnamed x37, local copies, waits for them, and re-layouts  9 us
    psum x1, blocking collectives, per_device(): squares = lax.psum(jnp.sum(linear_out * linear_out, axis=(1, 2)), 'head')  8.7 us
  transfers between devices with their start and end apart: 16, of which 6 were waited for; matrix products, arithmetic and copies ran while one was open for 10% of the time, Pallas kernels for 0%

commit v1 on v0

--- a/solution.py
+++ b/solution.py
@@ -146,7 +146,7 @@
         narrow("htu,uhd->thd", attend, values)
         + wide("thd,hde->the", query_wide, incoming) * carried_prev[:, None, None]
     )
-    squares = lax.psum(jnp.sum(linear_out * linear_out, axis=(1, 2)), "head")
+    squares = jnp.sum(lax.all_gather(jnp.sum(linear_out * linear_out, axis=(1, 2)), "head"), axis=0)
     inverse = lax.rsqrt(squares / features + norm_eps)
     mixed = (linear_out * inverse[:, None, None] * gain[None] + soft_out).astype(jnp.bfloat16)
     grad_wide = cotangent.astype(jnp.float32)

time: 235 us -> 241 us (1.026)
  blocking collectives: 8.7 us -> 13.9 us
  waiting for transfers between devices: 83.6 us -> 87 us
  starting transfers between devices: 95.2 us -> 91.9 us
    all_gather x0 -> x1, blocking collectives: none -> 5.23 us  [per_device(): lax.all_gather(jnp.sum(linear_out * linear_out, axis=(1, 2)), 'head')]
    ppermute x16, starting transfers between devices: 95.2 us -> 91.9 us  [from_behind(): return lax.ppermute(x, axis, pairs)]
    ppermute x16, waiting for transfers between devices: 83.6 us -> 87 us  [from_behind(): return lax.ppermute(x, axis, pairs)]
  transfers between devices with their start and end apart: 16 -> 16, of which waited for: 6 -> 6; matrix products, arithmetic and copies ran while one was open for 10% -> 9% of each run, Pallas kernels for 0% -> 0%
where the time goes in v1:
time: 241 us; the launch traced here: 240 us
  starting transfers between devices  91.9 us (38%)
  waiting for transfers between devices  87 us (36%)
  local copies, waits for them, and re-layouts  14.9 us (6%)
  matrix products  14.3 us (6%)
  blocking collectives  13.9 us (6%)
  between operations  10.3 us (4%)
  other arithmetic  7.3 us (3%)
    ppermute x16, starting transfers between devices, from_behind(): return lax.ppermute(x, axis, pairs)  91.9 us
    ppermute x16, waiting for transfers between devices, from_behind(): return lax.ppermute(x, axis, pairs)  87 us
    dot_general x27, matrix products, narrow(): return jnp.einsum(form, left, right, preferred_element_type=jnp.float32)  11.2 us
    unnamed x37, local copies, waits for them, and re-layouts  9 us
    psum x1, blocking collectives, per_device(): projection = lax.psum(jnp.sum(weighted * linear_out, axis=(1, 2)), 'head')  8.7 us
    all_gather x1, blocking collectives, per_device(): lax.all_gather(jnp.sum(linear_out * linear_out, axis=(1, 2)), 'head')  5.23 us
  transfers between devices with their start and end apart: 16, of which 6 were waited for; matrix products, arithmetic and copies ran while one was open for 9% of the time, Pallas kernels for 0%

profile of v1, /device:TPU:67, one launch (start us, length us, event | category | flops | bytes accessed | tf_op | source)
XLA Modules:
  0.0 239.6 jit_solution(568083190610898645)
XLA Ops:
  0.6 1.1 copy_bitcast_fusion
  1.8 0.8 pad_maximum_fusion
  2.6 3.1 %collective-permute-start.1 = (bf16[2,128,8,128]{3,1,2,0:T(8,128)(2,1)}, bf16[2,128,8,128]{3,1,2,0:T(8,128)(2,1)S(1)}, u32[]{:S(2)}, u32[]{:S(2)}) collective-permute-start(bf16[2,128,8,128]{3,1,2,0:T(8,128)(2,1)} %pad_maximum_fusion), channel_id=1, source_target_pairs={{0,8},{4,12},{8,16},{12,20},{16,24},{20,28},{24,32},{28,36},{32,40... | collective-permute-start | bytes 1572872 | tf_op jit(solution)/shard_map/ppermute | solution.py:15
  5.7 3.7 %collective-permute-start = (bf16[2,128,8,128]{3,1,2,0:T(8,128)(2,1)}, bf16[2,128,8,128]{3,1,2,0:T(8,128)(2,1)S(1)}, u32[]{:S(2)}, u32[]{:S(2)}) collective-permute-start(bf16[2,128,8,128]{3,1,2,0:T(8,128)(2,1)} %pad_maximum_fusion), channel_id=1, source_target_pairs={{0,4},{4,8},{8,12},{12,16},{16,20},{20,24},{24,28},{28,32},{32,36}... | collective-permute-start | bytes 1572872 | tf_op jit(solution)/shard_map/ppermute | solution.py:15
  9.5 0.6 copy-done.15
  10.4 0.7 fusion.105
  11.9 0.6 fusion.116
  13.2 1.2 compare_convert_fusion
  14.4 0.3 fusion.61
  14.8 3.2 %collective-permute-start.2 = (f32[8,128,128]{2,1,0:T(8,128)S(1)}, f32[8,128,128]{2,1,0:T(8,128)}, u32[]{:S(2)}, u32[]{:S(2)}) collective-permute-start(f32[8,128,128]{2,1,0:T(8,128)S(1)} %fusion.61), channel_id=1, source_target_pairs={{0,12},{4,16},{8,20},{12,24},{16,28},{20,32},{24,36},{28,40},{32,4... | collective-permute-start | bytes 1572872 | tf_op jit(solution)/shard_map/ppermute | solution.py:15
  18.0 0.7 slice.82
  18.8 0.6 slice.79
  20.1 0.6 fusion.118
  20.7 0.7 fusion.117
  21.5 0.7 fusion.115
  22.2 1.3 broadcast_compare_fusion.1
  23.5 0.7 fusion.114
  24.4 0.7 copy-done.1
  33.0 0.3 convolution_bitcast_fusion.4
  33.3 1.6 fusion.17
  35.0 0.4 fusion.19
  35.3 5.5 %collective-permute-start.3 = (f32[8,128,128]{2,1,0:T(8,128)S(1)}, f32[8,128,128]{2,1,0:T(8,128)S(1)}, u32[]{:S(2)}, u32[]{:S(2)}) collective-permute-start(f32[8,128,128]{2,1,0:T(8,128)S(1)} %fusion.19), channel_id=1, source_target_pairs={{0,4},{4,8},{8,12},{12,16},{16,20},{20,24},{24,28},{28,32},{32,36}... | collective-permute-start | bytes 1572872 | tf_op jit(solution)/shard_map/ppermute | solution.py:15
  40.8 5.5 %collective-permute-start.4 = (f32[8,128,128]{2,1,0:T(8,128)S(1)}, f32[8,128,128]{2,1,0:T(8,128)S(1)}, u32[]{:S(2)}, u32[]{:S(2)}) collective-permute-start(f32[8,128,128]{2,1,0:T(8,128)S(1)} %fusion.19), channel_id=1, source_target_pairs={{0,20},{4,24},{8,28},{12,32},{16,36},{20,40},{24,44},{28,48},{32,5... | collective-permute-start | bytes 1572872 | tf_op jit(solution)/shard_map/ppermute | solution.py:15
  46.4 12.2 %collective-permute-start.5 = (f32[8,128,128]{2,1,0:T(8,128)S(1)}, f32[8,128,128]{2,1,0:T(8,128)S(1)}, u32[]{:S(2)}, u32[]{:S(2)}) collective-permute-start(f32[8,128,128]{2,1,0:T(8,128)S(1)} %fusion.19), channel_id=1, source_target_pairs={{0,36},{4,40},{8,44},{12,48},{16,52},{20,56},{24,60},{28,64},{32,6... | collective-permute-start | bytes 1572872 | tf_op jit(solution)/shard_map/ppermute | solution.py:15
  58.5 1.9 collective-permute-start.6
  61.4 0.3 convolution_bitcast_fusion.3
  61.7 0.6 copy-done
  62.3 0.9 fusion.42
  63.3 0.9 fusion.41
  64.2 1.0 convolution_bitcast_fusion
  65.6 0.8 copy-done.7
  66.6 4.2 %collective-permute-done.5 = f32[8,128,128]{2,1,0:T(8,128)S(1)} collective-permute-done((f32[8,128,128]{2,1,0:T(8,128)S(1)}, f32[8,128,128]{2,1,0:T(8,128)S(1)}, u32[]{:S(2)}, u32[]{:S(2)}) %collective-permute-start.5) | collective-permute-done | bytes 524320 | tf_op jit(solution)/shard_map/ppermute | solution.py:15
  70.8 11.6 %collective-permute-done.6 = f32[8,128,128]{2,1,0:T(8,128)S(1)} collective-permute-done((f32[8,128,128]{2,1,0:T(8,128)S(1)}, f32[8,128,128]{2,1,0:T(8,128)S(1)}, u32[]{:S(2)}, u32[]{:S(2)}) %collective-permute-start.6) | collective-permute-done | bytes 524320 | tf_op jit(solution)/shard_map/ppermute | solution.py:15
  82.5 0.6 copy-done.14
  83.1 1.4 fusion.47
  84.5 8.7 %psum.7 = f32[128]{0:T(128)S(1)} all-reduce(f32[128]{0:T(128)S(1)} %get-tuple-element.20), channel_id=1, replica_groups=mesh['ctx'=64,'head'=4] {'head'}, use_global_device_ids=true, to_apply=%region_16.17 | all-reduce | flops 128 | bytes 1024 | tf_op jit(solution)/shard_map/psum | solution.py:154
  93.2 5.2 %all-gather.1 = f32[4,1,128]{2,1,0:T(1,128)S(1)} all-gather(f32[1,1,128]{2,1,0:T(1,128)S(1)} %bitcast.211), channel_id=2, replica_groups=mesh['ctx'=64,'head'=4] {'head'}, dimensions={0}, use_global_device_ids=true | all-gather | bytes 2560 | tf_op jit(solution)/shard_map/all_gather | solution.py:149
  98.4 1.3 fusion.46
  100.0 0.3 fusion.57
  100.4 8.0 %collective-permute-start.7 = (f32[8,128,128]{2,1,0:T(8,128)S(1)}, f32[8,128,128]{2,1,0:T(8,128)S(1)}, u32[]{:S(2)}, u32[]{:S(2)}) collective-permute-start(f32[8,128,128]{2,1,0:T(8,128)S(1)} %fusion.57), channel_id=1, source_target_pairs={{4,0},{8,4},{12,8},{16,12},{20,16},{24,20},{28,24},{32,28},{36,32}... | collective-permute-start | bytes 1572872 | tf_op jit(solution)/shard_map/ppermute | solution.py:15
  108.4 1.9 collective-permute-start.8
  110.3 18.0 %collective-permute-start.9 = (f32[8,128,128]{2,1,0:T(8,128)S(1)}, f32[8,128,128]{2,1,0:T(8,128)S(1)}, u32[]{:S(2)}, u32[]{:S(2)}) collective-permute-start(f32[8,128,128]{2,1,0:T(8,128)S(1)} %fusion.57), channel_id=1, source_target_pairs={{12,0},{16,4},{20,8},{24,12},{28,16},{32,20},{36,24},{40,28},{44,3... | collective-permute-start | bytes 1572872 | tf_op jit(solution)/shard_map/ppermute | solution.py:15
  128.6 0.7 fusion.27
  129.3 0.4 copy-done.8
  129.6 0.3 fusion.33
  130.2 0.7 copy-done.13
  131.0 2.1 collective-permute-start.15
  133.0 0.3 fusion.34
  133.6 0.7 copy-done.12
  134.4 2.3 collective-permute-start.14
  137.9 10.4 %collective-permute-done.9 = f32[8,128,128]{2,1,0:T(8,128)S(1)} collective-permute-done((f32[8,128,128]{2,1,0:T(8,128)S(1)}, f32[8,128,128]{2,1,0:T(8,128)S(1)}, u32[]{:S(2)}, u32[]{:S(2)}) %collective-permute-start.9) | collective-permute-done | bytes 524320 | tf_op jit(solution)/shard_map/ppermute | solution.py:15
  148.4 6.6 %collective-permute-start.10 = (f32[8,128,128]{2,1,0:T(8,128)S(1)}, f32[8,128,128]{2,1,0:T(8,128)S(1)}, u32[]{:S(2)}, u32[]{:S(2)}) collective-permute-start(f32[8,128,128]{2,1,0:T(8,128)S(1)} %multiply_add_fusion.1), channel_id=1, source_target_pairs={{4,0},{8,4},{12,8},{16,12},{20,16},{24,20},{28,24},{32,28},{36,32}... | collective-permute-start | bytes 1572872 | tf_op jit(solution)/shard_map/ppermute | solution.py:15
  155.0 14.0 %collective-permute-start.11 = (f32[8,128,128]{2,1,0:T(8,128)S(1)}, f32[8,128,128]{2,1,0:T(8,128)S(1)}, u32[]{:S(2)}, u32[]{:S(2)}) collective-permute-start(f32[8,128,128]{2,1,0:T(8,128)S(1)} %multiply_add_fusion.1), channel_id=1, source_target_pairs={{20,0},{24,4},{28,8},{32,12},{36,16},{40,20},{44,24},{48,28},{52,3... | collective-permute-start | bytes 1572872 | tf_op jit(solution)/shard_map/ppermute | solution.py:15
  168.9 1.9 collective-permute-start.12
  170.9 2.1 collective-permute-start.13
  173.2 0.9 copy.282
  174.1 0.9 copy.283
  175.6 7.1 %collective-permute-done.10 = f32[8,128,128]{2,1,0:T(8,128)S(1)} collective-permute-done((f32[8,128,128]{2,1,0:T(8,128)S(1)}, f32[8,128,128]{2,1,0:T(8,128)S(1)}, u32[]{:S(2)}, u32[]{:S(2)}) %collective-permute-start.10) | collective-permute-done | bytes 524320 | tf_op jit(solution)/shard_map/ppermute | solution.py:15
  182.7 26.1 %collective-permute-done.11 = f32[8,128,128]{2,1,0:T(8,128)S(1)} collective-permute-done((f32[8,128,128]{2,1,0:T(8,128)S(1)}, f32[8,128,128]{2,1,0:T(8,128)S(1)}, u32[]{:S(2)}, u32[]{:S(2)}) %collective-permute-start.11) | collective-permute-done | bytes 524320 | tf_op jit(solution)/shard_map/ppermute | solution.py:15
  208.8 27.6 %collective-permute-done.13 = f32[8,128,128]{2,1,0:T(8,128)S(1)} collective-permute-done((f32[8,128,128]{2,1,0:T(8,128)S(1)}, f32[8,128,128]{2,1,0:T(8,128)S(1)}, u32[]{:S(2)}, u32[]{:S(2)}) %collective-permute-start.13) | collective-permute-done | bytes 524320 | tf_op jit(solution)/shard_map/ppermute | solution.py:15
  236.5 0.7 fusion.31
  237.3 0.9 copy.284
  238.3 0.4 fusion.32
  238.7 0.9 copy.285
  (85 shorter events, 7.2 us)
Async XLA Ops:
  1.8 12.6 %copy-start.2 = (bf16[128,8,128]{2,1,0:T(8,128)(2,1)S(1)}, bf16[128,8,128]{2,1,0:T(8,128)(2,1)}, u32[]{:S(2)}) copy-start(bf16[128,8,128]{2,1,0:T(8,128)(2,1)} %param.8) | copy-start | bytes 786436
  1.8 12.6 %copy-start.3 = (bf16[128,8,128]{2,1,0:T(8,128)(2,1)S(1)}, bf16[128,8,128]{2,1,0:T(8,128)(2,1)}, u32[]{:S(2)}) copy-start(bf16[128,8,128]{2,1,0:T(8,128)(2,1)} %param.7) | copy-start | bytes 786436
  2.6 30.7 %collective-permute-start.1 = (bf16[2,128,8,128]{3,1,2,0:T(8,128)(2,1)}, bf16[2,128,8,128]{3,1,2,0:T(8,128)(2,1)S(1)}, u32[]{:S(2)}, u32[]{:S(2)}) collective-permute-start(bf16[2,128,8,128]{3,1,2,0:T(8,128)(2,1)} %pad_maximum_fusion), channel_id=1, source_target_pairs={{0,8},{4,12},{8,16},{12,20},{16,24},{20,28},{24,32},{28,36},{32,40... | collective-permute-start | bytes 1572872 | tf_op jit(solution)/shard_map/ppermute | solution.py:15
  5.7 29.2 %collective-permute-start = (bf16[2,128,8,128]{3,1,2,0:T(8,128)(2,1)}, bf16[2,128,8,128]{3,1,2,0:T(8,128)(2,1)S(1)}, u32[]{:S(2)}, u32[]{:S(2)}) collective-permute-start(bf16[2,128,8,128]{3,1,2,0:T(8,128)(2,1)} %pad_maximum_fusion), channel_id=1, source_target_pairs={{0,4},{4,8},{8,12},{12,16},{16,20},{20,24},{24,28},{28,32},{32,36}... | collective-permute-start | bytes 1572872 | tf_op jit(solution)/shard_map/ppermute | solution.py:15
  9.4 0.7 copy-start.15
  14.8 18.6 %collective-permute-start.2 = (f32[8,128,128]{2,1,0:T(8,128)S(1)}, f32[8,128,128]{2,1,0:T(8,128)}, u32[]{:S(2)}, u32[]{:S(2)}) collective-permute-start(f32[8,128,128]{2,1,0:T(8,128)S(1)} %fusion.61), channel_id=1, source_target_pairs={{0,12},{4,16},{8,20},{12,24},{16,28},{20,32},{24,36},{28,40},{32,4... | collective-permute-start | bytes 1572872 | tf_op jit(solution)/shard_map/ppermute | solution.py:15
  24.1 1.0 copy-start.1
  33.3 27.1 %copy-start.6 = (bf16[2,128,8,128]{3,1,2,0:T(8,128)(2,1)}, bf16[2,128,8,128]{3,1,2,0:T(8,128)(2,1)S(1)}, u32[]{:S(2)}) copy-start(bf16[2,128,8,128]{3,1,2,0:T(8,128)(2,1)S(1)} %collective-permute-done.1) | copy-start | bytes 1572868
  34.9 30.3 %copy-start.9 = (bf16[2,128,8,128]{3,1,2,0:T(8,128)(2,1)}, bf16[2,128,8,128]{3,1,2,0:T(8,128)(2,1)S(1)}, u32[]{:S(2)}) copy-start(bf16[2,128,8,128]{3,1,2,0:T(8,128)(2,1)S(1)} %collective-permute-done) | copy-start | bytes 1572868
  35.3 31.3 %collective-permute-start.3 = (f32[8,128,128]{2,1,0:T(8,128)S(1)}, f32[8,128,128]{2,1,0:T(8,128)S(1)}, u32[]{:S(2)}, u32[]{:S(2)}) collective-permute-start(f32[8,128,128]{2,1,0:T(8,128)S(1)} %fusion.19), channel_id=1, source_target_pairs={{0,4},{4,8},{8,12},{12,16},{16,20},{20,24},{24,28},{28,32},{32,36}... | collective-permute-start | bytes 1572872 | tf_op jit(solution)/shard_map/ppermute | solution.py:15
  40.8 25.8 %collective-permute-start.4 = (f32[8,128,128]{2,1,0:T(8,128)S(1)}, f32[8,128,128]{2,1,0:T(8,128)S(1)}, u32[]{:S(2)}, u32[]{:S(2)}) collective-permute-start(f32[8,128,128]{2,1,0:T(8,128)S(1)} %fusion.19), channel_id=1, source_target_pairs={{0,20},{4,24},{8,28},{12,32},{16,36},{20,40},{24,44},{28,48},{32,5... | collective-permute-start | bytes 1572872 | tf_op jit(solution)/shard_map/ppermute | solution.py:15
  46.4 24.5 %collective-permute-start.5 = (f32[8,128,128]{2,1,0:T(8,128)S(1)}, f32[8,128,128]{2,1,0:T(8,128)S(1)}, u32[]{:S(2)}, u32[]{:S(2)}) collective-permute-start(f32[8,128,128]{2,1,0:T(8,128)S(1)} %fusion.19), channel_id=1, source_target_pairs={{0,36},{4,40},{8,44},{12,48},{16,52},{20,56},{24,60},{28,64},{32,6... | collective-permute-start | bytes 1572872 | tf_op jit(solution)/shard_map/ppermute | solution.py:15
  58.5 23.9 %collective-permute-start.6 = (f32[8,128,128]{2,1,0:T(8,128)S(1)}, f32[8,128,128]{2,1,0:T(8,128)S(1)}, u32[]{:S(2)}, u32[]{:S(2)}) collective-permute-start(f32[8,128,128]{2,1,0:T(8,128)S(1)} %fusion.19), channel_id=1, source_target_pairs={{0,52},{4,56},{8,60},{12,64},{16,68},{20,72},{24,76},{28,80},{32,8... | collective-permute-start | bytes 1572872 | tf_op jit(solution)/shard_map/ppermute | solution.py:15
  61.4 1.0 copy-start
  65.3 1.0 copy-start.7
  82.4 0.7 copy-start.14
  82.5 1.9 copy-start.4
  100.4 28.2 %copy-start.5 = (f32[8,128,128]{2,1,0:T(8,128)S(1)}, f32[8,128,128]{2,1,0:T(8,128)}, u32[]{:S(2)}) copy-start(f32[8,128,128]{2,1,0:T(8,128)} %copy-done.4) | copy-start | bytes 1572868
  100.4 37.5 %collective-permute-start.7 = (f32[8,128,128]{2,1,0:T(8,128)S(1)}, f32[8,128,128]{2,1,0:T(8,128)S(1)}, u32[]{:S(2)}, u32[]{:S(2)}) collective-permute-start(f32[8,128,128]{2,1,0:T(8,128)S(1)} %fusion.57), channel_id=1, source_target_pairs={{4,0},{8,4},{12,8},{16,12},{20,16},{24,20},{28,24},{32,28},{36,32}... | collective-permute-start | bytes 1572872 | tf_op jit(solution)/shard_map/ppermute | solution.py:15
  108.4 29.5 %collective-permute-start.8 = (f32[8,128,128]{2,1,0:T(8,128)S(1)}, f32[8,128,128]{2,1,0:T(8,128)S(1)}, u32[]{:S(2)}, u32[]{:S(2)}) collective-permute-start(f32[8,128,128]{2,1,0:T(8,128)S(1)} %fusion.57), channel_id=1, source_target_pairs={{8,0},{12,4},{16,8},{20,12},{24,16},{28,20},{32,24},{36,28},{40,32... | collective-permute-start | bytes 1572872 | tf_op jit(solution)/shard_map/ppermute | solution.py:15
  110.3 37.9 %collective-permute-start.9 = (f32[8,128,128]{2,1,0:T(8,128)S(1)}, f32[8,128,128]{2,1,0:T(8,128)S(1)}, u32[]{:S(2)}, u32[]{:S(2)}) collective-permute-start(f32[8,128,128]{2,1,0:T(8,128)S(1)} %fusion.57), channel_id=1, source_target_pairs={{12,0},{16,4},{20,8},{24,12},{28,16},{32,20},{36,24},{40,28},{44,3... | collective-permute-start | bytes 1572872 | tf_op jit(solution)/shard_map/ppermute | solution.py:15
  128.6 1.0 copy-start.8
  130.0 1.0 copy-start.13
  130.9 2.1 copy-start.10
  131.0 39.9 %collective-permute-start.15 = (bf16[2,128,8,128]{3,1,2,0:T(8,128)(2,1)S(1)}, bf16[2,128,8,128]{3,1,2,0:T(8,128)(2,1)S(1)}, u32[]{:S(2)}, u32[]{:S(2)}) collective-permute-start(bf16[2,128,8,128]{3,1,2,0:T(8,128)(2,1)S(1)} %pad_maximum_fusion.2), channel_id=1, source_target_pairs={{8,0},{12,4},{16,8},{20,12},{24,16},{28,20},{32,24},{36,28},{40,32... | collective-permute-start | bytes 1572872 | tf_op jit(solution)/shard_map/ppermute | solution.py:15
  133.4 1.0 copy-start.12
  134.4 41.1 %collective-permute-start.14 = (bf16[2,128,8,128]{3,1,2,0:T(8,128)(2,1)S(1)}, bf16[2,128,8,128]{3,1,2,0:T(8,128)(2,1)S(1)}, u32[]{:S(2)}, u32[]{:S(2)}) collective-permute-start(bf16[2,128,8,128]{3,1,2,0:T(8,128)(2,1)S(1)} %pad_maximum_fusion.1), channel_id=1, source_target_pairs={{4,0},{8,4},{12,8},{16,12},{20,16},{24,20},{28,24},{32,28},{36,32}... | collective-permute-start | bytes 1572872 | tf_op jit(solution)/shard_map/ppermute | solution.py:15
  148.4 34.3 %collective-permute-start.10 = (f32[8,128,128]{2,1,0:T(8,128)S(1)}, f32[8,128,128]{2,1,0:T(8,128)S(1)}, u32[]{:S(2)}, u32[]{:S(2)}) collective-permute-start(f32[8,128,128]{2,1,0:T(8,128)S(1)} %multiply_add_fusion.1), channel_id=1, source_target_pairs={{4,0},{8,4},{12,8},{16,12},{20,16},{24,20},{28,24},{32,28},{36,32}... | collective-permute-start | bytes 1572872 | tf_op jit(solution)/shard_map/ppermute | solution.py:15
  155.0 53.8 %collective-permute-start.11 = (f32[8,128,128]{2,1,0:T(8,128)S(1)}, f32[8,128,128]{2,1,0:T(8,128)S(1)}, u32[]{:S(2)}, u32[]{:S(2)}) collective-permute-start(f32[8,128,128]{2,1,0:T(8,128)S(1)} %multiply_add_fusion.1), channel_id=1, source_target_pairs={{20,0},{24,4},{28,8},{32,12},{36,16},{40,20},{44,24},{48,28},{52,3... | collective-permute-start | bytes 1572872 | tf_op jit(solution)/shard_map/ppermute | solution.py:15
  168.9 39.9 %collective-permute-start.12 = (f32[8,128,128]{2,1,0:T(8,128)S(1)}, f32[8,128,128]{2,1,0:T(8,128)S(1)}, u32[]{:S(2)}, u32[]{:S(2)}) collective-permute-start(f32[8,128,128]{2,1,0:T(8,128)S(1)} %multiply_add_fusion.1), channel_id=1, source_target_pairs={{36,0},{40,4},{44,8},{48,12},{52,16},{56,20},{60,24},{64,28},{68,3... | collective-permute-start | bytes 1572872 | tf_op jit(solution)/shard_map/ppermute | solution.py:15
  170.9 65.5 %collective-permute-start.13 = (f32[8,128,128]{2,1,0:T(8,128)S(1)}, f32[8,128,128]{2,1,0:T(8,128)S(1)}, u32[]{:S(2)}, u32[]{:S(2)}) collective-permute-start(f32[8,128,128]{2,1,0:T(8,128)S(1)} %multiply_add_fusion.1), channel_id=1, source_target_pairs={{52,0},{56,4},{60,8},{64,12},{68,16},{72,20},{76,24},{80,28},{84,3... | collective-permute-start | bytes 1572872 | tf_op jit(solution)/shard_map/ppermute | solution.py:15
  237.2 1.0 copy-start.11
